TPU v7x, 512 devices: a whole 4x8x8 slice. The times are simulated.
512 devices in a mesh: dp: 8 (over z), cent: 64 (over x, y, core).
Axes of the slice: x: 4, y: 8, z: 8, core: 2. Of those that a mesh axis runs over, the one named last changes fastest.
Arguments:
- points: bfloat16 [24576, 1024], P(('dp', 'cent')), may hold values from -6 to 6
- assign: int32 [24576], P(('dp', 'cent')), may hold values from 0 to 32767, as said below
- centroids: float32 [32768, 1024], P('cent'), may hold values from -6 to 6
- counts: int32 [32768], P('cent'), may hold values from 1 to 4
Outputs:
- new_centroids: float32 [32768, 1024], P('cent')
- best: float32 [24576], P(('dp', 'cent'))
Inputs may be any that keep to these rules, and one draw needn't show every extreme that they name: `assign`: split the points into aligned blocks of 3072 points in order (the points of one dp index). In every block, the clusters k * 512 to (k + 1) * 512 - 1 receive exactly 48 points together, for every k.
All inputs are finite; a program needn't handle non-finite values.
Results may differ from a plain program's by a relative error of at most 0.0003.
Values may be sent and summed in bfloat16 or wider, within the bound.
No kernel may reach another device: no remote copies, remote signals or barrier semaphores. Data moves between devices by JAX's collectives and lax.ppermute only.
A program may use at most 128 MiB of HBM per device.

v0:
```python
import jax
import jax.numpy as jnp
from jax import lax
from jax.sharding import PartitionSpec as P


def renorm(merged):
    return merged * lax.rsqrt(jnp.mean(merged * merged, axis=1, keepdims=True) + 1e-05)


def cluster_terms(rows, labels, kdev):
    first = lax.axis_index("cent") * kdev
    local = labels - first
    onehot = (local[None, :] == jnp.arange(kdev, dtype=jnp.int32)[:, None]).astype(jnp.bfloat16)
    return jnp.dot(onehot, rows, preferred_element_type=jnp.float32)


def per_device(points, assign, centroids, counts):
    kdev = centroids.shape[0]
    pdev = points.shape[0]
    weighted = centroids * counts.astype(jnp.float32)[:, None]
    rows, labels = (
        lax.all_gather(points, "cent", axis=0, tiled=True),
        lax.all_gather(assign, "cent", axis=0, tiled=True),
    )
    sums = cluster_terms(rows, labels, kdev)
    total = lax.psum(sums, "dp")
    fresh = renorm(weighted + total)
    rounded = fresh.astype(jnp.bfloat16)
    scores = jnp.dot(rows, rounded.T, preferred_element_type=jnp.float32)
    local_best = jnp.max(scores, axis=1)
    merged_best = lax.pmax(local_best, "cent")
    top = lax.dynamic_slice_in_dim(merged_best, lax.axis_index("cent") * pdev, pdev, 0)
    values = points.astype(jnp.float32)
    width = points.shape[1]
    scale = width * jnp.sqrt(jnp.mean(values * values, axis=1) + 1e-06)
    return (fresh, top / scale)


def solution(mesh):
    placed = (P(("dp", "cent"), None), P(("dp", "cent")), P("cent", None), P("cent"))
    return jax.shard_map(
        per_device,
        mesh=mesh,
        in_specs=placed,
        out_specs=(P("cent", None), P(("dp", "cent"))),
        check_vma=False,
    )
```

profile of v0, /device:TPU:64, one launch (start us, length us, event | category | flops | bytes accessed | tf_op | source)
XLA Modules:
  0.0 617.8 jit_solution(2940238520247544569)
XLA Ops:
  7.2 0.0 all-gather.2.cloned.1.call-start
  7.2 0.7 all-gather.2.cloned.1.call-update
  7.9 0.0 all-reduce.3.cloned.1.call-start
  7.9 1.3 dynamic-slice
  9.9 0.9 dynamic-update-slice
  10.8 251.6 %all-reduce = s32[3072]{0:T(1024)S(1)} all-reduce(s32[3072]{0:T(1024)S(1)} %dynamic-update-slice), channel_id=1, replica_groups=mesh['dp'=8,'cent'=64] {'cent'}, use_global_device_ids=true, to_apply=%add | all-reduce | flops 3072 | bytes 24576
  262.4 0.0 all-gather.2.cloned.1.call-done
  262.4 0.0 copy-start.3
  262.4 7.5 %fusion = f32[512,1024]{1,0:T(8,128)} fusion(bf16[3072,1024]{1,0:T(8,128)(2,1)} %all-gather.2.cloned.1.call-done, s32[3072]{0:T(1024)S(1)} %broadcast_subtract_fusion), kind=kOutput, calls=%fused_computation.1 | convolution fusion | flops 3222798336 | bytes 8400896 | tf_op jit(solution)/shard_map/dot_general | solution.py:15
  269.9 0.0 all-reduce.3.cloned.1.call-update
  269.9 0.7 copy-done.4
  270.6 0.0 copy-done.3
  270.6 0.1 multiply_reduce_fusion.1
  270.7 83.2 %all-reduce.3.cloned.1.call-done = f32[512,1024]{1,0:T(8,128)} async-done(((f32[512,1024]{1,0:T(8,128)}), f32[512,1024]{1,0:T(8,128)}) %all-reduce.3.cloned.1.call-update) | async-done | bytes 2097168 | tf_op jit(solution)/shard_map/psum | solution.py:27
  353.9 0.0 copy-done
  353.9 2.2 multiply_reduce_fusion
  356.1 0.1 copy-done.1
  356.1 0.4 broadcast_multiply_fusion
  356.5 0.0 copy-start.2
  356.5 1.3 copy-done.2
  357.8 1.8 copy-done.5
  359.7 3.7 convolution_reduce_fusion
  363.4 247.0 %pmax.7 = f32[3072]{0:T(1024)S(1)} all-reduce(f32[3072]{0:T(1024)S(1)} %convolution_reduce_fusion), channel_id=1, replica_groups=mesh['dp'=8,'cent'=64] {'cent'}, use_global_device_ids=true, to_apply=%region_3.0 | all-reduce | flops 3072 | bytes 24576 | tf_op jit(solution)/shard_map/pmax | solution.py:32
  610.4 0.6 multiply_divide_fusion
  (8 shorter events, 0.0 us)
Async XLA Ops:
  7.2 255.2 %all-gather.2.cloned.1.call-start = ((), (), s32[]{:S(2)}) async-start(), calls=%async_computation | async-start | bytes 6389760 | tf_op jit(solution)/shard_map/all_gather | solution.py:23
  7.9 346.0 %all-reduce.3.cloned.1.call-start = ((), (), s32[]{:S(2)}) async-start(), calls=%async_computation.1 | async-start | bytes 4194304 | tf_op jit(solution)/shard_map/psum | solution.py:27
  262.4 8.2 %copy-start.3 = (bf16[48,1024]{1,0:T(8,128)(2,1)S(1)}, bf16[48,1024]{1,0:T(8,128)(2,1)}, u32[]{:S(2)}) copy-start(bf16[48,1024]{1,0:T(8,128)(2,1)} %param.4) | copy-start | bytes 294916
  269.9 0.7 copy-start.4
  269.9 84.0 %copy-start = (f32[512,1024]{1,0:T(8,128)S(1)}, f32[512,1024]{1,0:T(8,128)}, u32[]{:S(2)}) copy-start(f32[512,1024]{1,0:T(8,128)} %param.6) | copy-start | bytes 6291460
  353.9 2.2 copy-start.1
  356.1 3.5 copy-start.5
  356.5 1.3 copy-start.2
Sparse Core Ops, SparseCore 0:
  11.3 89.7 all-gather.1
  270.1 83.7 all-reduce.2
where the time goes:
time: 618 us
  blocking collectives  499 us (81%)
  waiting for transfers between devices  83.9 us (14%)
  between operations  14.7 us (2%)
  matrix products  11.3 us (2%)
    unnamed x1, blocking collectives  252 us
    pmax x1, blocking collectives, per_device(): merged_best = lax.pmax(local_best, 'cent')  247 us
    psum x1, waiting for transfers between devices, per_device(): total = lax.psum(sums, 'dp')  83.2 us
  transfers between devices with their start and end apart: 2, of which 1 were waited for; matrix products, arithmetic and copies ran while one was open for 0% of the time, Pallas kernels for 0%

commit v1 on v0

--- a/solution.py
+++ b/solution.py
@@ -24,7 +24,9 @@
         lax.all_gather(assign, "cent", axis=0, tiled=True),
     )
     sums = cluster_terms(rows, labels, kdev)
-    total = lax.psum(sums, "dp")
+    total = sums
+    for hop in (1, 2, 4):
+        total = total + lax.ppermute(total, "dp", [(dev, dev ^ hop) for dev in range(8)])
     fresh = renorm(weighted + total)
     rounded = fresh.astype(jnp.bfloat16)
     scores = jnp.dot(rows, rounded.T, preferred_element_type=jnp.float32)

time: 618 us -> 773 us (1.25)
  the two profiles are of different devices: /device:TPU:64 before, /device:TPU:192 now
where the time goes in v1:
time: 773 us; the launch traced here: 772 us
  blocking collectives  505 us (65%)
  waiting for transfers between devices  221 us (29%)
  between operations  14.8 us (2%)
  matrix products  12.7 us (2%)
  starting transfers between devices  12.2 us (2%)
    pmax x1, blocking collectives, per_device(): merged_best = lax.pmax(local_best, 'cent')  253 us
    unnamed x1, blocking collectives  252 us
    ppermute x3, waiting for transfers between devices, per_device(): lax.ppermute(total, 'dp', [(dev, dev ^ hop) for dev in range(8)])  221 us
  transfers between devices with their start and end apart: 4, of which 3 were waited for; matrix products, arithmetic and copies ran while one was open for 0% of the time, Pallas kernels for 0%

profile of v1, /device:TPU:192, one launch (start us, length us, event | category | flops | bytes accessed | tf_op | source)
XLA Modules:
  0.0 772.2 jit_solution(5320542348832728749)
XLA Ops:
  7.2 0.0 all-gather.2.cloned.1.call-start
  7.2 0.7 all-gather.2.cloned.1.call-update
  7.9 1.3 dynamic-slice
  9.8 0.9 dynamic-update-slice
  10.7 251.6 %all-reduce = s32[3072]{0:T(1024)S(1)} all-reduce(s32[3072]{0:T(1024)S(1)} %dynamic-update-slice), channel_id=1, replica_groups=mesh['dp'=8,'cent'=64] {'cent'}, use_global_device_ids=true, to_apply=%add | all-reduce | flops 3072 | bytes 24576
  262.3 5.5 fusion
  267.8 1.9 collective-permute-start
  269.7 42.4 %collective-permute-done = f32[512,1024]{1,0:T(8,128)S(1)} collective-permute-done((f32[512,1024]{1,0:T(8,128)S(1)}, f32[512,1024]{1,0:T(8,128)S(1)}, u32[]{:S(2)}, u32[]{:S(2)}) %collective-permute-start) | collective-permute-done | bytes 2097184 | tf_op jit(solution)/shard_map/ppermute | solution.py:29
  312.1 0.4 add.32
  312.5 0.0 copy-start.2
  312.5 0.0 copy-start.1
  312.5 2.1 collective-permute-start.1
  314.6 87.3 %collective-permute-done.1 = f32[512,1024]{1,0:T(8,128)S(1)} collective-permute-done((f32[512,1024]{1,0:T(8,128)S(1)}, f32[512,1024]{1,0:T(8,128)S(1)}, u32[]{:S(2)}, u32[]{:S(2)}) %collective-permute-start.1) | collective-permute-done | bytes 2097184 | tf_op jit(solution)/shard_map/ppermute | solution.py:29
  401.9 0.4 add.33
  402.3 8.2 %collective-permute-start.2 = (f32[512,1024]{1,0:T(8,128)S(1)}, f32[512,1024]{1,0:T(8,128)}, u32[]{:S(2)}, u32[]{:S(2)}) collective-permute-start(f32[512,1024]{1,0:T(8,128)S(1)} %add.33), channel_id=1, source_target_pairs={{0,256},{64,320},{128,384},{192,448},{256,0},{320,64},{384,128},{4... | collective-permute-start | bytes 6291464 | tf_op jit(solution)/shard_map/ppermute | solution.py:29
  410.5 0.0 copy-done.2
  410.5 0.1 multiply_reduce_fusion.1
  410.6 90.8 %collective-permute-done.2 = f32[512,1024]{1,0:T(8,128)} collective-permute-done((f32[512,1024]{1,0:T(8,128)S(1)}, f32[512,1024]{1,0:T(8,128)}, u32[]{:S(2)}, u32[]{:S(2)}) %collective-permute-start.2) | collective-permute-done | bytes 2097184 | tf_op jit(solution)/shard_map/ppermute | solution.py:29
  501.5 2.7 multiply_reduce_fusion
  504.2 0.2 broadcast_multiply_fusion
  504.4 0.0 copy-start
  504.4 7.2 convolution_reduce_fusion
  511.7 253.0 %pmax.7 = f32[3072]{0:T(1024)S(1)} all-reduce(f32[3072]{0:T(1024)S(1)} %convolution_reduce_fusion), channel_id=1, replica_groups=mesh['dp'=8,'cent'=64] {'cent'}, use_global_device_ids=true, to_apply=%region_2.0 | all-reduce | flops 3072 | bytes 24576 | tf_op jit(solution)/shard_map/pmax | solution.py:34
  764.7 0.6 multiply_divide_fusion
  (7 shorter events, 0.0 us)
Async XLA Ops:
  7.2 255.1 %all-gather.2.cloned.1.call-start = ((), (), s32[]{:S(2)}) async-start(), calls=%async_computation | async-start | bytes 6389760 | tf_op jit(solution)/shard_map/all_gather | solution.py:23
  267.8 44.3 %collective-permute-start = (f32[512,1024]{1,0:T(8,128)S(1)}, f32[512,1024]{1,0:T(8,128)S(1)}, u32[]{:S(2)}, u32[]{:S(2)}) collective-permute-start(f32[512,1024]{1,0:T(8,128)S(1)} %fusion), channel_id=1, source_target_pairs={{0,64},{64,0},{128,192},{192,128},{256,320},{320,256},{384,448},{4... | collective-permute-start | bytes 6291464 | tf_op jit(solution)/shard_map/ppermute | solution.py:29
  312.5 98.0 %copy-start.2 = (s32[512]{0:T(512)S(1)}, s32[512]{0:T(512)}, u32[]{:S(2)}) copy-start(s32[512]{0:T(512)} %param.7) | copy-start | bytes 6148
  312.5 98.0 %copy-start.1 = (bf16[48,1024]{1,0:T(8,128)(2,1)S(1)}, bf16[48,1024]{1,0:T(8,128)(2,1)}, u32[]{:S(2)}) copy-start(bf16[48,1024]{1,0:T(8,128)(2,1)} %param.4) | copy-start | bytes 294916
  312.5 89.4 %collective-permute-start.1 = (f32[512,1024]{1,0:T(8,128)S(1)}, f32[512,1024]{1,0:T(8,128)S(1)}, u32[]{:S(2)}, u32[]{:S(2)}) collective-permute-start(f32[512,1024]{1,0:T(8,128)S(1)} %add.32), channel_id=1, source_target_pairs={{0,128},{64,192},{128,0},{192,64},{256,384},{320,448},{384,256},{4... | collective-permute-start | bytes 6291464 | tf_op jit(solution)/shard_map/ppermute | solution.py:29
  402.3 99.2 %collective-permute-start.2 = (f32[512,1024]{1,0:T(8,128)S(1)}, f32[512,1024]{1,0:T(8,128)}, u32[]{:S(2)}, u32[]{:S(2)}) collective-permute-start(f32[512,1024]{1,0:T(8,128)S(1)} %add.33), channel_id=1, source_target_pairs={{0,256},{64,320},{128,384},{192,448},{256,0},{320,64},{384,128},{4... | collective-permute-start | bytes 6291464 | tf_op jit(solution)/shard_map/ppermute | solution.py:29
  504.4 7.3 copy-start
Sparse Core Ops, SparseCore 0:
  11.3 88.3 all-gather.1
